TPU v7x, 32 devices: a whole 2x2x4 slice. The times are simulated.
32 devices in a mesh: groups: 2 (over y), tiles: 4 (over z), sections: 2 (over x), chan: 2 (over core).
Axes of the slice: x: 2, y: 2, z: 4, core: 2. Of those that a mesh axis runs over, the one named last changes fastest.
Arguments:
- features: bfloat16 [8, 16, 64, 1024], P('groups', ('tiles', 'chan')), parts along dimension 0, may hold values from -6 to 6
- tissue: int32 [8, 16, 64], P('groups', ('tiles', 'chan')), parts along dimension 0, may hold values from 0 to 1, as said below
- row_label: int32 [8, 16], P('groups', ('tiles', 'chan')), parts along dimension 0, may hold values from 0 to 1
- prototypes: bfloat16 [2, 1024], replicated, may hold values from -5 to 5
- reduce_weight: bfloat16 [2, 1024, 256], P('sections', 'chan'), may hold values from -0.1875 to 0.1875
- spatial_weight: bfloat16 [2, 3, 3, 256, 256], P('sections', None, None, None, 'chan'), may hold values from -0.125 to 0.125
- expand_weight: bfloat16 [2, 256, 1024], P('sections', None, 'chan'), may hold values from -0.375 to 0.375
- norm_gain: float32 [2, 2, 256], P('sections'), may hold values from 0.25 to 1.75
- norm_bias: float32 [2, 2, 256], P('sections'), may hold values from -3 to 3
Outputs:
- grad_reduce: bfloat16 [4, 1024, 256], P(('groups', 'sections'), 'chan'), parts along dimension 0
- grad_spatial: bfloat16 [4, 3, 3, 256, 256], P(('groups', 'sections'), None, None, None, 'chan'), parts along dimension 0
- grad_expand: bfloat16 [4, 256, 1024], P(('groups', 'sections'), None, 'chan'), parts along dimension 0
- grad_gain: float32 [4, 2, 256], P(('groups', 'sections'), None, 'chan'), parts along dimension 0
- grad_bias: float32 [4, 2, 256], P(('groups', 'sections'), None, 'chan'), parts along dimension 0
There are 2 independent parts, one for each index of `groups`. A program takes and returns all parts, laid end to end along the dimension named above; an argument that names none is the same for every part. Nothing has to cross between parts.
Inputs may be any that keep to these rules, and one draw needn't show every extreme that they name: 1 marks a tissue cell, 0 background.
All inputs are finite; a program needn't handle non-finite values.
Results may differ from a plain program's by a relative error of at most 0.011.
Values may be sent and summed in bfloat16 or wider, within the bound.
No kernel may reach another device: no remote copies, remote signals or barrier semaphores. Data moves between devices by JAX's collectives and lax.ppermute only.
A program may use at most 128 MiB of HBM per device.

v0:
```python
import functools
import jax
import jax.numpy as jnp
from jax import lax
from jax.sharding import PartitionSpec as P

ROW_AXES = ("tiles", "chan")


def halo_rows(block):
    count = lax.axis_size(ROW_AXES)
    forward = [(i, i + 1) for i in range(count - 1)]
    backward = [(target, source) for source, target in forward]
    low = lax.ppermute(block[:, -1:], ROW_AXES, forward)
    high = lax.ppermute(block[:, :1], ROW_AXES, backward)
    return jnp.concatenate([low, block, high], axis=1)


def grid_taps(extended, height, breadth, mirrored):
    padded = jnp.pad(extended, ((0, 0), (0, 0), (1, 1), (0, 0)))
    tap_list = []
    for shift_row in range(3):
        for shift_col in range(3):
            if mirrored:
                start_row = 2 - shift_row
                start_col = 2 - shift_col
            else:
                start_row = shift_row
                start_col = shift_col
            tap_list.append(
                padded[:, start_row : start_row + height, start_col : start_col + breadth]
            )
    stacked = jnp.concatenate(tap_list, axis=3)
    return stacked.reshape(extended.shape[0] * height * breadth, stacked.shape[3])


def gather_blocks(half, chan_axis, chain, position):
    received = [
        lax.ppermute(half, "sections", [(i, (i + k) % chain) for i in range(chain)])
        for k in range(1, chain)
    ]
    stacked = jnp.stack([half] + received)
    if chan_axis is not None:
        stacked = lax.all_gather(stacked, "chan", axis=chan_axis + 1, tiled=True)
    return [
        lax.dynamic_index_in_dim(stacked, (position - b + chain) % chain, 0, keepdims=False)
        for b in range(chain)
    ]


def weight_partials(ops, cells, height, breadth):
    cur, h1e, h2, reduced, spatial_out, grad_block, masked_two, grad_two, masked_one, grad_one = ops
    full = cur.shape[-1]
    inner = h2.shape[-1]
    block_flat = grad_block.reshape(cells, full)
    two_flat = grad_two.reshape(cells, inner)
    one_flat = grad_one.reshape(cells, inner)
    reduce_term = jnp.dot(
        cur.reshape(cells, full).T, one_flat, preferred_element_type=jnp.float32
    ).astype(jnp.bfloat16)
    spatial_term = jnp.dot(
        grid_taps(h1e, height, breadth, False).T, two_flat, preferred_element_type=jnp.float32
    ).astype(jnp.bfloat16)
    expand_term = jnp.dot(
        h2.reshape(cells, inner).T, block_flat, preferred_element_type=jnp.float32
    ).astype(jnp.bfloat16)
    gain = jnp.stack(
        [
            jnp.sum(masked_one * reduced, axis=(0, 1, 2)),
            jnp.sum(masked_two * spatial_out, axis=(0, 1, 2)),
        ]
    )
    bias = jnp.stack([jnp.sum(masked_one, axis=(0, 1, 2)), jnp.sum(masked_two, axis=(0, 1, 2))])
    small = jnp.concatenate([gain, bias]).astype(jnp.bfloat16)
    return (
        reduce_term.reshape(2, full // 2, inner),
        spatial_term.reshape(9 * inner, 2, inner // 2).transpose(1, 0, 2),
        expand_term.reshape(inner, 2, full // 2).transpose(1, 0, 2),
        small.reshape(4, 2, inner // 2).transpose(1, 0, 2),
    )


def local(
    features,
    tissue,
    row_label,
    prototypes,
    reduce_weight,
    spatial_weight,
    expand_weight,
    norm_gain,
    norm_bias,
):
    regions, height, breadth, full_width = features.shape
    chain = lax.axis_size("sections")
    position = lax.axis_index("sections")
    chan_index = lax.axis_index("chan")
    reduce_all = gather_blocks(reduce_weight[0], 0, chain, position)
    spatial_all = gather_blocks(spatial_weight[0], 3, chain, position)
    expand_all = gather_blocks(expand_weight[0], 1, chain, position)
    gain_all = gather_blocks(norm_gain[0], None, chain, position)
    bias_all = gather_blocks(norm_bias[0], None, chain, position)
    inner_width = reduce_all[0].shape[1]
    tissue_mask = tissue.astype(jnp.float32)[:, :, :, None]
    cells = regions * height * breadth
    inner_shape = (regions, height, breadth, inner_width)
    outer_shape = (regions, height, breadth, full_width)
    current = features
    saved = []
    for b in range(chain):
        gain_pair, bias_pair = (gain_all[b], bias_all[b])
        reduced = jnp.dot(
            current.reshape(cells, full_width), reduce_all[b], preferred_element_type=jnp.float32
        ).reshape(inner_shape)
        pre_reduce = gain_pair[0] * reduced + bias_pair[0]
        hidden_one = jnp.maximum(pre_reduce, 0.0).astype(jnp.bfloat16)
        hidden_ext = halo_rows(hidden_one)
        spatial_out = jnp.dot(
            grid_taps(hidden_ext, height, breadth, False),
            spatial_all[b].reshape(9 * inner_width, inner_width),
            preferred_element_type=jnp.float32,
        ).reshape(inner_shape)
        pre_spatial = gain_pair[1] * spatial_out + bias_pair[1]
        hidden_two = jnp.maximum(pre_spatial, 0.0).astype(jnp.bfloat16)
        expanded = jnp.dot(
            hidden_two.reshape(cells, inner_width),
            expand_all[b],
            preferred_element_type=jnp.float32,
        ).reshape(outer_shape)
        block_out = (tissue_mask * jnp.maximum(current.astype(jnp.float32) + expanded, 0.0)).astype(
            jnp.bfloat16
        )
        saved.append(
            (
                current,
                hidden_ext,
                reduced,
                pre_reduce,
                spatial_out,
                pre_spatial,
                hidden_two,
                block_out,
            )
        )
        current = block_out
    classes = prototypes.shape[0]
    chosen = (row_label[:, :, None] == jnp.arange(classes, dtype=jnp.int32)).astype(jnp.float32)
    target_rows = jnp.einsum("mrk,kc->mrc", chosen, prototypes.astype(jnp.float32))
    total_cells = regions * height * lax.axis_size("tiles") * lax.axis_size("chan") * breadth
    upstream = (
        tissue_mask * (current.astype(jnp.float32) - target_rows[:, :, None, :]) / total_cells
    ).astype(jnp.bfloat16)
    block_ops = [None] * chain
    for b in reversed(range(chain)):
        (
            block_in,
            hidden_ext,
            reduced,
            pre_reduce,
            spatial_out,
            pre_spatial,
            hidden_two,
            block_out,
        ) = saved[b]
        needed = b >= position
        gain_pair = gain_all[b]

        def first_back(
            upstream=upstream,
            block_out=block_out,
            pre_spatial=pre_spatial,
            b=b,
            gain_pair=gain_pair,
        ):
            grad_block = jnp.where(block_out > 0, upstream, jnp.zeros_like(upstream))
            back_two = jnp.dot(
                grad_block.reshape(cells, full_width),
                expand_all[b].T,
                preferred_element_type=jnp.float32,
            ).reshape(inner_shape)
            masked_two = jnp.where(pre_spatial > 0, back_two, jnp.float32(0.0))
            grad_two = (masked_two * gain_pair[1]).astype(jnp.bfloat16)
            return (grad_block, masked_two, grad_two)

        def first_skip():
            return (
                jnp.zeros(outer_shape, jnp.bfloat16),
                jnp.zeros(inner_shape, jnp.float32),
                jnp.zeros(inner_shape, jnp.bfloat16),
            )

        grad_block, masked_two, grad_two = lax.cond(needed, first_back, first_skip)
        grad_ext = halo_rows(grad_two)

        def second_back(grad_ext=grad_ext, pre_reduce=pre_reduce, b=b, gain_pair=gain_pair):
            back_one = jnp.dot(
                grid_taps(grad_ext, height, breadth, True),
                jnp.transpose(spatial_all[b], (0, 1, 3, 2)).reshape(9 * inner_width, inner_width),
                preferred_element_type=jnp.float32,
            ).reshape(inner_shape)
            masked_one = jnp.where(pre_reduce > 0, back_one, jnp.float32(0.0))
            grad_one = (masked_one * gain_pair[0]).astype(jnp.bfloat16)
            return (masked_one, grad_one)

        def second_skip():
            return (jnp.zeros(inner_shape, jnp.float32), jnp.zeros(inner_shape, jnp.bfloat16))

        masked_one, grad_one = lax.cond(needed, second_back, second_skip)
        block_ops[b] = (
            block_in,
            hidden_ext,
            hidden_two,
            reduced,
            spatial_out,
            grad_block,
            masked_two,
            grad_two,
            masked_one,
            grad_one,
        )
        if b > 0:

            def pass_back(grad_block=grad_block, grad_one=grad_one, b=b):
                return (
                    grad_block.astype(jnp.float32)
                    + jnp.dot(
                        grad_one.reshape(cells, inner_width),
                        reduce_all[b].T,
                        preferred_element_type=jnp.float32,
                    ).reshape(outer_shape)
                ).astype(jnp.bfloat16)

            upstream = lax.cond(
                b > position, pass_back, lambda: jnp.zeros(outer_shape, jnp.bfloat16)
            )
    partials = lax.switch(
        position,
        [
            functools.partial(lambda k: weight_partials(block_ops[k], cells, height, breadth), k)
            for k in range(chain)
        ],
    )
    totals = []
    for piece in partials:
        mine = lax.dynamic_index_in_dim(piece, chan_index, 0, keepdims=False)
        theirs = lax.dynamic_index_in_dim(piece, 1 - chan_index, 0, keepdims=False)
        arrived = lax.ppermute(theirs, "chan", [(0, 1), (1, 0)])
        pair_sum = (mine.astype(jnp.float32) + arrived.astype(jnp.float32)).astype(jnp.bfloat16)
        totals.append(lax.psum(pair_sum, "tiles"))
    half_inner = inner_width // 2
    grad_reduce = totals[0][None]
    grad_spatial = totals[1].reshape(3, 3, inner_width, half_inner)[None]
    grad_expand = totals[2][None]
    small = totals[3].astype(jnp.float32)
    return (grad_reduce, grad_spatial, grad_expand, small[0:2][None], small[2:4][None])


def solution(mesh):
    placed = (
        P("groups", ("tiles", "chan"), None, None),
        P("groups", ("tiles", "chan"), None),
        P("groups", ("tiles", "chan")),
        P(),
        P("sections", "chan", None),
        P("sections", None, None, None, "chan"),
        P("sections", None, "chan"),
        P("sections", None, None),
        P("sections", None, None),
    )
    return jax.shard_map(
        local,
        mesh=mesh,
        in_specs=placed,
        out_specs=(
            P(("groups", "sections"), "chan", None),
            P(("groups", "sections"), None, None, None, "chan"),
            P(("groups", "sections"), None, "chan"),
            P(("groups", "sections"), None, "chan"),
            P(("groups", "sections"), None, "chan"),
        ),
        check_vma=False,
    )
```

profile of v0, /device:TPU:0, one launch (start us, length us, event | category | flops | bytes accessed | tf_op | source)
XLA Modules:
  0.0 206.3 jit_solution(13812828813498507578)
XLA Ops:
  7.2 3.0 %collective-permute-start.1 = (bf16[512,256]{1,0:T(8,128)(2,1)}, bf16[512,256]{1,0:T(8,128)(2,1)S(1)}, u32[]{:S(2)}, u32[]{:S(2)}) collective-permute-start(bf16[512,256]{1,0:T(8,128)(2,1)} %bitcast.257), channel_id=1, source_target_pairs={{0,2},{2,0},{1,3},{3,1},{4,6},{6,4},{5,7},{7,5},{8,10},{10,8},{9,1... | collective-permute-start | bytes 786440 | tf_op jit(solution)/shard_map/ppermute | solution.py:39
  10.3 6.5 %collective-permute-done.1 = bf16[512,256]{1,0:T(8,128)(2,1)S(1)} collective-permute-done((bf16[512,256]{1,0:T(8,128)(2,1)}, bf16[512,256]{1,0:T(8,128)(2,1)S(1)}, u32[]{:S(2)}, u32[]{:S(2)}) %collective-permute-start.1) | collective-permute-done | bytes 262176 | tf_op jit(solution)/shard_map/ppermute | solution.py:39
  22.0 12.8 %collective-permute-done.5 = bf16[3,3,256,128]{2,3,1,0:T(8,128)(2,1)S(1)} collective-permute-done((bf16[3,3,256,128]{2,3,1,0:T(8,128)(2,1)S(1)}, bf16[3,3,256,128]{2,3,1,0:T(8,128)(2,1)S(1)}, u32[]{:S(2)}, u32[]{:S(2)}) %collective-permute-start.5) | collective-permute-done | bytes 589856 | tf_op jit(solution)/shard_map/ppermute | solution.py:39
  47.4 2.8 %collective-permute-done.4 = bf16[4,1,64,256]{3,2,1,0:T(8,128)(2,1)S(1)} collective-permute-done((bf16[4,1,64,256]{3,2,1,0:T(8,128)(2,1)S(1)}, bf16[4,1,64,256]{3,2,1,0:T(8,128)(2,1)S(1)}, u32[]{:S(2)}, u32[]{:S(2)}) %collective-permute-start.4) | collective-permute-done | bytes 131104 | tf_op jit(solution)/shard_map/ppermute | solution.py:15
  57.3 3.0 %constant_dynamic-slice_fusion.6 = (bf16[1,3,3,256,256]{3,4,2,1,0:T(8,128)(2,1)}, bf16[1,3,3,256,256]{3,4,2,1,0:T(8,128)(2,1)S(1)}) fusion(bf16[2,3,3,256,256]{3,4,2,1,0:T(8,128)(2,1)} %all-gather.6.cloned.1.call-done, s32[]{:T(128)S(6)} %select_n.84, s32[]{:T(128)S(6)} %select_n.82), kind=kLoop, calls=%fused_computation.185 | loop fusion | bytes 4718600 | tf_op jit(solution)/shard_map/jit(dynamic_index_in_dim)/dynamic_slice | solution.py:46
  61.8 3.6 %maximum_convert_fusion.2 = (bf16[4,2,64,256]{3,2,1,0:T(8,128)(2,1)}, f32[4,2,64,256]{3,2,1,0:T(8,128)S(1)}, f32[4,2,64,256]{3,2,1,0:T(8,128)}) fusion(f32[256]{0:T(256)S(1)} %bitcast.263, f32[256]{0:T(256)S(1)} %bitcast.264, bf16[4,2,64,2304]{3,2,1,0:T(8,128)(2,1)} %fusion.50, bf16[2304,256,1,1]{1,0,3,2:T(8,128)(2,1)} %bitcast.246), kind=kOutput, calls=%fused_computation.127 | convolution fusion | flops 604504064 | bytes 4851712 | tf_op jit(solution)/shard_map/dot_general | solution.py:118
  65.5 2.1 %multiply_convert_fusion.6 = bf16[4,2,64,1024]{3,2,1,0:T(8,128)(2,1)S(1)} fusion(bf16[4,2,64,1024]{3,2,1,0:T(8,128)(2,1)} %param.21, f32[4,2,64]{2,1,0:T(2,128)S(1)} %convert_element_type.145, bf16[2,256,1024]{2,1,0:T(8,128)(2,1)} %all-gather.8.cloned.1.call-done, s32[]{:T(128)S(6)} %select_n.82, f32[4,2,64,256]{3,2,1,0:T(8,128)S(1)} %get-tuple-element.187), kind=kOutput, calls=%fused_computation.102 | convolution fusion | flops 271319040 | bytes 3147780 | tf_op jit(solution)/shard_map/dot_general | solution.py:125
  68.9 5.3 %collective-permute-start.7 = (bf16[4,1,64,256]{3,2,1,0:T(8,128)(2,1)S(1)}, bf16[4,1,64,256]{3,2,1,0:T(8,128)(2,1)S(1)}, u32[]{:S(2)}, u32[]{:S(2)}) collective-permute-start(bf16[4,1,64,256]{3,2,1,0:T(8,128)(2,1)S(1)} %get-tuple-element.212), channel_id=1, source_target_pairs={{0,1},{1,4},{4,5},{5,8},{8,9},{9,12},{12,13},{2,3},{3,6},{6,7},{7,... | collective-permute-start | bytes 393224 | tf_op jit(solution)/shard_map/ppermute | solution.py:14
  76.6 2.4 %copy.28 = bf16[1,3,3,256,256]{4,3,2,1,0:T(8,128)(2,1)} copy(bf16[1,3,3,256,256]{3,4,2,1,0:T(8,128)(2,1)} %get-tuple-element.204) | data formatting | bytes 2359296 | tf_op jit(solution)/shard_map/jit(dynamic_index_in_dim)/dynamic_slice | solution.py:46
  85.7 3.6 %conditional.6 = (bf16[4,2,64,1024]{3,2,1,0:T(8,128)(2,1)}, f32[4,2,64,256]{3,2,1,0:T(8,128)}, bf16[4,2,64,256]{3,2,1,0:T(8,128)(2,1)S(1)}) conditional(s32[]{:T(128)} %convert_element_type.151, () %tuple.57, (bf16[4,2,64,1024]{3,2,1,0:T(8,128)(2,1)S(1)}, bf16[4,2,64,1024]{3,2,1,0:T(8,128)(2,1)S(1)}, f32[4,2,64,256]{3,2,1,0:T(8,128)S(1)}, ...), branch_computations={%region_0.1_spmd, %region_1.2_spmd} | conditional | flops 270008320 | bytes 6032408 | solution.py:192
  86.7 2.6 %multiply_convert_fusion = (bf16[4,2,64,256]{3,2,1,0:T(8,128)(2,1)S(1)}, f32[4,2,64,256]{3,2,1,0:T(8,128)}) fusion(f32[256]{0:T(256)S(1)} %bitcast.271, bf16[4,2,64,1024]{3,2,1,0:T(8,128)(2,1)} %compare_select_fusion, bf16[256,1024]{1,0:T(8,128)(2,1)S(1)} %get-tuple-element.90, f32[4,2,64,256]{3,2,1,0:T(8,128)S(1)} %get-tuple-element.89), kind=kOutput, calls=%fused_computation.3 | convolution fusion | flops 268959744 | bytes 2884608 | tf_op jit(solution)/shard_map/cond/branch_1_fun/dot_general | solution.py:176
  90.0 3.7 %collective-permute-start.9 = (bf16[4,1,64,256]{3,2,1,0:T(8,128)(2,1)}, bf16[4,1,64,256]{3,2,1,0:T(8,128)(2,1)}, u32[]{:S(2)}, u32[]{:S(2)}) collective-permute-start(bf16[4,1,64,256]{3,2,1,0:T(8,128)(2,1)} %get-tuple-element.210), channel_id=1, source_target_pairs={{0,1},{1,4},{4,5},{5,8},{8,9},{9,12},{12,13},{2,3},{3,6},{6,7},{7,... | collective-permute-start | bytes 393224 | tf_op jit(solution)/shard_map/ppermute | solution.py:14
  98.2 3.1 %conditional.7 = (f32[4,2,64,256]{3,2,1,0:T(8,128)}, bf16[4,2,64,256]{3,2,1,0:T(8,128)(2,1)S(1)}) conditional(s32[]{:T(128)} %convert_element_type.151, () %tuple.59, (f32[4,2,64,256]{3,2,1,0:T(8,128)}, bf16[4,4,64,256]{3,2,1,0:T(8,128)(2,1)S(1)}, bf16[1,3,3,256,256]{3,4,2,1,0:T(8,128)(2,1)}, f32[2,256]{1,0:T(2,128)S(1)}) %tuple.139), branch_computations={%region_2.3_spmd, %region_3.4_spmd} | conditional | flops 604504064 | bytes 17960008 | solution.py:208
  101.9 2.9 %conditional.8 = (bf16[4,2,64,1024]{3,2,1,0:T(8,128)(2,1)}) conditional(s32[]{:T(128)} %convert_element_type.150, () %tuple.56, (bf16[4,2,64,1024]{3,2,1,0:T(8,128)(2,1)}, bf16[4,2,64,256]{3,2,1,0:T(8,128)(2,1)S(1)}, bf16[1024,256]{1,0:T(8,128)(2,1)}) %tuple.61), branch_computations={%region_4.5_spmd, %region_5.6_spmd} | conditional | flops 270008320 | bytes 2883592 | solution.py:233
  101.9 2.9 %add_convert_fusion = bf16[4,2,64,1024]{3,2,1,0:T(8,128)(2,1)} fusion(bf16[4,2,64,1024]{3,2,1,0:T(8,128)(2,1)} %get-tuple-element.96, bf16[4,2,64,256]{3,2,1,0:T(8,128)(2,1)S(1)} %get-tuple-element.97, bf16[1024,256]{1,0:T(8,128)(2,1)} %get-tuple-element.98), kind=kOutput, calls=%fused_computation.21 | convolution fusion | flops 270008320 | bytes 2883584 | tf_op jit(solution)/shard_map/cond/branch_1_fun/dot_general | solution.py:226
  104.8 4.2 %conditional.9 = (bf16[4,2,64,1024]{3,2,1,0:T(8,128)(2,1)}, f32[4,2,64,256]{3,2,1,0:T(8,128)S(1)}, bf16[4,2,64,256]{3,2,1,0:T(8,128)(2,1)S(1)}) conditional(s32[]{:T(128)} %convert_element_type.144, () %tuple.55, (bf16[4,2,64,1024]{3,2,1,0:T(8,128)(2,1)S(1)}, bf16[4,2,64,1024]{3,2,1,0:T(8,128)(2,1)}, f32[4,2,64,256]{3,2,1,0:T(8,128)}, ...), branch_computations={%region_6.7_spmd, %region_7.8_spmd} | conditional | flops 270008320 | bytes 10226768 | solution.py:192
  104.8 2.5 %compare_select_fusion.1 = bf16[4,2,64,1024]{3,2,1,0:T(8,128)(2,1)} fusion(bf16[4,2,64,1024]{3,2,1,0:T(8,128)(2,1)} %get-tuple-element.100, bf16[4,2,64,1024]{3,2,1,0:T(8,128)(2,1)S(1)} %get-tuple-element.99), kind=kLoop, calls=%fused_computation.23 | loop fusion | flops 1048576 | bytes 3145728 | tf_op jit(solution)/shard_map/cond/branch_1_fun/jit(_where)/select_n | solution.py:175
  110.4 6.1 %collective-permute-start.11 = (bf16[4,1,64,256]{3,2,1,0:T(8,128)(2,1)}, bf16[4,1,64,256]{3,2,1,0:T(8,128)(2,1)}, u32[]{:S(2)}, u32[]{:S(2)}) collective-permute-start(bf16[4,1,64,256]{3,2,1,0:T(8,128)(2,1)} %get-tuple-element.208), channel_id=1, source_target_pairs={{0,1},{1,4},{4,5},{5,8},{8,9},{9,12},{12,13},{2,3},{3,6},{6,7},{7,... | collective-permute-start | bytes 393224 | tf_op jit(solution)/shard_map/ppermute | solution.py:14
  120.9 2.5 %conditional.10 = (f32[4,2,64,256]{3,2,1,0:T(8,128)S(1)}, bf16[4,2,64,256]{3,2,1,0:T(8,128)(2,1)S(1)}) conditional(s32[]{:T(128)} %convert_element_type.144, () %tuple.54, (f32[4,2,64,256]{3,2,1,0:T(8,128)}, bf16[4,4,64,256]{3,2,1,0:T(8,128)(2,1)S(1)}, bf16[1,3,3,256,256]{3,4,2,1,0:T(8,128)(2,1)}, f32[2,256]{1,0:T(2,128)S(1)}) %tuple.137), branch_computations={%region_8.9_spmd, %region_9.10_spmd} | conditional | flops 604504064 | bytes 17960008 | solution.py:208
  123.4 8.0 %conditional.11 = (bf16[2,512,256]{2,1,0:T(8,128)(2,1)}, bf16[2,2304,128]{1,2,0:T(8,128)(2,1)S(1)}, bf16[2,4,128]{2,0,1:T(2,128)(2,1)S(1)}, bf16[2,256,512]{2,1,0:T(8,128)(2,1)S(1)}, bf16[2,4,128]{2,1,0:T(4,128)(2,1)S(1)}) conditional(s32[]{:T(128)} %clamp.3, (bf16[4,2,64,1024]{3,2,1,0:T(8,128)(2,1)}, bf16[4,2,64,256]{3,2,1,0:T(8,128)(2,1)S(1)}, ...), branch_computations={%region_10.15_spmd, %region_15.20_spmd} | conditional | flops 1142753280 | bytes 23226548 | solution.py:236
  125.0 2.5 %fusion.16 = bf16[1024,256]{1,0:T(8,128)(2,1)} fusion(bf16[4,2,64,1024]{3,2,1,0:T(8,128)(2,1)} %get-tuple-element.108, bf16[4,2,64,256]{3,2,1,0:T(8,128)(2,1)S(1)} %get-tuple-element.109), kind=kOutput, calls=%fused_computation.48 | convolution fusion | flops 268697600 | bytes 1835008 | tf_op jit(solution)/shard_map/cond/branch_0_fun/dot_general | solution.py:58
  131.5 2.5 %collective-permute-start.15 = (bf16[256,512]{1,0:T(8,128)(2,1)S(1)}, bf16[256,512]{1,0:T(8,128)(2,1)}, u32[]{:S(2)}, u32[]{:S(2)}) collective-permute-start(bf16[256,512]{1,0:T(8,128)(2,1)S(1)} %dynamic-slice_bitcast_fusion.4), channel_id=1, source_target_pairs={{0,1},{1,0},{2,3},{3,2},{4,5},{5,4},{6,7},{7,6},{8,9},{9,8},{10,11... | collective-permute-start | bytes 786440 | tf_op jit(solution)/shard_map/ppermute | solution.py:247
  142.3 10.8 %psum.31 = bf16[4,128]{1,0:T(4,128)(2,1)S(1)} all-reduce(bf16[4,128]{1,0:T(4,128)(2,1)S(1)} %fusion.73), channel_id=1, replica_groups=mesh['groups'=2,'tiles'=4,'sections'=2,'chan'=2] {'tiles'}, use_global_device_ids=true, to_apply=%region_23.24 | all-reduce | flops 512 | bytes 2048 | tf_op jit(solution)/shard_map/psum | solution.py:249
  153.6 40.9 %all-reduce.9.cloned.1.call-done = (bf16[1,512,256]{2,1,0:T(8,128)(2,1)}, bf16[1,3,3,256,128]{4,3,2,1,0:T(8,128)(2,1)}, bf16[1,256,512]{2,1,0:T(8,128)(2,1)}) async-done(((bf16[1,512,256]{2,1,0:T(8,128)(2,1)}, bf16[1,3,3,256,128]{4,3,2,1,0:T(8,128)(2,1)}, bf16[1,256,512]{2,1,0:T(8,128)(2,1)}), (bf16[1,512,256]{2,1,0:T(8,128)(2,1)}, bf16[1,3,3,256,128]{4,3,2,1,0:T(8,128)(2,1)}, ...) | async-done | bytes 1114128 | tf_op jit(solution)/shard_map/psum | solution.py:249
  (208 shorter events, 75.7 us)
Async XLA Ops:
  7.2 32.5 %copy-start = (bf16[2,1024]{1,0:T(2,128)(2,1)S(1)}, bf16[2,1024]{1,0:T(2,128)(2,1)}, u32[]{:S(2)}) copy-start(bf16[2,1024]{1,0:T(2,128)(2,1)} %param.24) | copy-start | bytes 12292
  7.2 34.0 %all-gather.4.cloned.1.call-start = ((), (), s32[]{:S(2)}) async-start(), calls=%async_computation | async-start | bytes 1572864 | tf_op jit(solution)/shard_map/all_gather | solution.py:44
  7.2 9.5 %collective-permute-start.1 = (bf16[512,256]{1,0:T(8,128)(2,1)}, bf16[512,256]{1,0:T(8,128)(2,1)S(1)}, u32[]{:S(2)}, u32[]{:S(2)}) collective-permute-start(bf16[512,256]{1,0:T(8,128)(2,1)} %bitcast.257), channel_id=1, source_target_pairs={{0,2},{2,0},{1,3},{3,1},{4,6},{6,4},{5,7},{7,5},{8,10},{10,8},{9,1... | collective-permute-start | bytes 786440 | tf_op jit(solution)/shard_map/ppermute | solution.py:39
  18.7 22.5 %copy-start.18 = (bf16[4,2,64,1024]{3,2,1,0:T(8,128)(2,1)S(1)}, bf16[4,2,64,1024]{3,2,1,0:T(8,128)(2,1)}, u32[]{:S(2)}) copy-start(bf16[4,2,64,1024]{3,2,1,0:T(8,128)(2,1)} %param.21) | copy-start | bytes 3145732
  18.7 38.7 %all-gather.6.cloned.1.call-start = ((), (), s32[]{:S(2)}) async-start(), calls=%async_computation.1 | async-start | bytes 3538944 | tf_op jit(solution)/shard_map/all_gather | solution.py:44
  20.2 14.6 %collective-permute-start.5 = (bf16[3,3,256,128]{2,3,1,0:T(8,128)(2,1)S(1)}, bf16[3,3,256,128]{2,3,1,0:T(8,128)(2,1)S(1)}, u32[]{:S(2)}, u32[]{:S(2)}) collective-permute-start(bf16[3,3,256,128]{2,3,1,0:T(8,128)(2,1)S(1)} %bitcast.248), channel_id=1, source_target_pairs={{0,2},{2,0},{1,3},{3,1},{4,6},{6,4},{5,7},{7,5},{8,10},{10,8},{9,1... | collective-permute-start | bytes 1769480 | tf_op jit(solution)/shard_map/ppermute | solution.py:39
  35.9 29.6 %all-gather.8.cloned.1.call-start = ((), (), s32[]{:S(2)}) async-start(), calls=%async_computation.2 | async-start | bytes 1572864 | tf_op jit(solution)/shard_map/all_gather | solution.py:44
  36.0 4.5 %collective-permute-start.2 = (f32[2,256]{1,0:T(2,128)S(1)}, f32[2,256]{1,0:T(2,128)S(1)}, u32[]{:S(2)}, u32[]{:S(2)}) collective-permute-start(f32[2,256]{1,0:T(2,128)S(1)} %bitcast.284), channel_id=1, source_target_pairs={{0,2},{2,0},{1,3},{3,1},{4,6},{6,4},{5,7},{7,5},{8,10},{10,8},{9,1... | collective-permute-start | bytes 6152 | tf_op jit(solution)/shard_map/ppermute | solution.py:39
  37.5 3.6 %collective-permute-start = (f32[2,256]{1,0:T(2,128)S(1)}, f32[2,256]{1,0:T(2,128)S(1)}, u32[]{:S(2)}, u32[]{:S(2)}) collective-permute-start(f32[2,256]{1,0:T(2,128)S(1)} %bitcast.283), channel_id=1, source_target_pairs={{0,2},{2,0},{1,3},{3,1},{4,6},{6,4},{5,7},{7,5},{8,10},{10,8},{9,1... | collective-permute-start | bytes 6152 | tf_op jit(solution)/shard_map/ppermute | solution.py:39
  38.1 8.4 %collective-permute-start.6 = (bf16[256,512]{1,0:T(8,128)(2,1)S(1)}, bf16[256,512]{1,0:T(8,128)(2,1)S(1)}, u32[]{:S(2)}, u32[]{:S(2)}) collective-permute-start(bf16[256,512]{1,0:T(8,128)(2,1)S(1)} %bitcast.258), channel_id=1, source_target_pairs={{0,2},{2,0},{1,3},{3,1},{4,6},{6,4},{5,7},{7,5},{8,10},{10,8},{9,1... | collective-permute-start | bytes 786440 | tf_op jit(solution)/shard_map/ppermute | solution.py:39
  40.4 25.1 %copy-start.32 = (f32[4,2,64]{2,1,0:T(2,128)}, f32[4,2,64]{2,1,0:T(2,128)S(1)}, u32[]{:S(2)}) copy-start(f32[4,2,64]{2,1,0:T(2,128)S(1)} %convert_element_type.145) | copy-start | bytes 6148
  43.9 3.6 %collective-permute-start.3 = (bf16[4,1,64,256]{3,2,1,0:T(8,128)(2,1)S(1)}, bf16[4,1,64,256]{3,2,1,0:T(8,128)(2,1)S(1)}, u32[]{:S(2)}, u32[]{:S(2)}) collective-permute-start(bf16[4,1,64,256]{3,2,1,0:T(8,128)(2,1)S(1)} %get-tuple-element.214), channel_id=1, source_target_pairs={{0,1},{1,4},{4,5},{5,8},{8,9},{9,12},{12,13},{2,3},{3,6},{6,7},{7,... | collective-permute-start | bytes 393224 | tf_op jit(solution)/shard_map/ppermute | solution.py:14
  45.2 5.0 %collective-permute-start.4 = (bf16[4,1,64,256]{3,2,1,0:T(8,128)(2,1)S(1)}, bf16[4,1,64,256]{3,2,1,0:T(8,128)(2,1)S(1)}, u32[]{:S(2)}, u32[]{:S(2)}) collective-permute-start(bf16[4,1,64,256]{3,2,1,0:T(8,128)(2,1)S(1)} %get-tuple-element.215), channel_id=1, source_target_pairs={{1,0},{4,1},{5,4},{8,5},{9,8},{12,9},{13,12},{3,2},{6,3},{7,6},{10... | collective-permute-start | bytes 393224 | tf_op jit(solution)/shard_map/ppermute | solution.py:15
  47.4 147.1 %all-reduce.9.cloned.1.call-start = ((), (), s32[]{:S(2)}) async-start(), calls=%async_computation.3 | async-start | bytes 2228224 | tf_op jit(solution)/shard_map/psum | solution.py:249
  68.9 10.1 %collective-permute-start.7 = (bf16[4,1,64,256]{3,2,1,0:T(8,128)(2,1)S(1)}, bf16[4,1,64,256]{3,2,1,0:T(8,128)(2,1)S(1)}, u32[]{:S(2)}, u32[]{:S(2)}) collective-permute-start(bf16[4,1,64,256]{3,2,1,0:T(8,128)(2,1)S(1)} %get-tuple-element.212), channel_id=1, source_target_pairs={{0,1},{1,4},{4,5},{5,8},{8,9},{9,12},{12,13},{2,3},{3,6},{6,7},{7,... | collective-permute-start | bytes 393224 | tf_op jit(solution)/shard_map/ppermute | solution.py:14
  74.2 5.4 %collective-permute-start.8 = (bf16[4,1,64,256]{3,2,1,0:T(8,128)(2,1)S(1)}, bf16[4,1,64,256]{3,2,1,0:T(8,128)(2,1)S(1)}, u32[]{:S(2)}, u32[]{:S(2)}) collective-permute-start(bf16[4,1,64,256]{3,2,1,0:T(8,128)(2,1)S(1)} %get-tuple-element.213), channel_id=1, source_target_pairs={{1,0},{4,1},{5,4},{8,5},{9,8},{12,9},{13,12},{3,2},{6,3},{7,6},{10... | collective-permute-start | bytes 393224 | tf_op jit(solution)/shard_map/ppermute | solution.py:15
  90.0 6.9 %collective-permute-start.9 = (bf16[4,1,64,256]{3,2,1,0:T(8,128)(2,1)}, bf16[4,1,64,256]{3,2,1,0:T(8,128)(2,1)}, u32[]{:S(2)}, u32[]{:S(2)}) collective-permute-start(bf16[4,1,64,256]{3,2,1,0:T(8,128)(2,1)} %get-tuple-element.210), channel_id=1, source_target_pairs={{0,1},{1,4},{4,5},{5,8},{8,9},{9,12},{12,13},{2,3},{3,6},{6,7},{7,... | collective-permute-start | bytes 393224 | tf_op jit(solution)/shard_map/ppermute | solution.py:14
  93.6 3.5 %collective-permute-start.10 = (bf16[4,1,64,256]{3,2,1,0:T(8,128)(2,1)S(1)}, bf16[4,1,64,256]{3,2,1,0:T(8,128)(2,1)}, u32[]{:S(2)}, u32[]{:S(2)}) collective-permute-start(bf16[4,1,64,256]{3,2,1,0:T(8,128)(2,1)S(1)} %get-tuple-element.211), channel_id=1, source_target_pairs={{1,0},{4,1},{5,4},{8,5},{9,8},{12,9},{13,12},{3,2},{6,3},{7,6},{10... | collective-permute-start | bytes 393224 | tf_op jit(solution)/shard_map/ppermute | solution.py:15
  110.4 7.4 %collective-permute-start.11 = (bf16[4,1,64,256]{3,2,1,0:T(8,128)(2,1)}, bf16[4,1,64,256]{3,2,1,0:T(8,128)(2,1)}, u32[]{:S(2)}, u32[]{:S(2)}) collective-permute-start(bf16[4,1,64,256]{3,2,1,0:T(8,128)(2,1)} %get-tuple-element.208), channel_id=1, source_target_pairs={{0,1},{1,4},{4,5},{5,8},{8,9},{9,12},{12,13},{2,3},{3,6},{6,7},{7,... | collective-permute-start | bytes 393224 | tf_op jit(solution)/shard_map/ppermute | solution.py:14
  116.5 3.4 %collective-permute-start.12 = (bf16[4,1,64,256]{3,2,1,0:T(8,128)(2,1)S(1)}, bf16[4,1,64,256]{3,2,1,0:T(8,128)(2,1)}, u32[]{:S(2)}, u32[]{:S(2)}) collective-permute-start(bf16[4,1,64,256]{3,2,1,0:T(8,128)(2,1)S(1)} %get-tuple-element.209), channel_id=1, source_target_pairs={{1,0},{4,1},{5,4},{8,5},{9,8},{12,9},{13,12},{3,2},{6,3},{7,6},{10... | collective-permute-start | bytes 393224 | tf_op jit(solution)/shard_map/ppermute | solution.py:15
  131.5 4.6 %collective-permute-start.15 = (bf16[256,512]{1,0:T(8,128)(2,1)S(1)}, bf16[256,512]{1,0:T(8,128)(2,1)}, u32[]{:S(2)}, u32[]{:S(2)}) collective-permute-start(bf16[256,512]{1,0:T(8,128)(2,1)S(1)} %dynamic-slice_bitcast_fusion.4), channel_id=1, source_target_pairs={{0,1},{1,0},{2,3},{3,2},{4,5},{5,4},{6,7},{7,6},{8,9},{9,8},{10,11... | collective-permute-start | bytes 786440 | tf_op jit(solution)/shard_map/ppermute | solution.py:247
  134.1 5.7 %collective-permute-start.14 = (bf16[2304,128]{0,1:T(8,128)(2,1)S(1)}, bf16[2304,128]{0,1:T(8,128)(2,1)S(1)}, u32[]{:S(2)}, u32[]{:S(2)}) collective-permute-start(bf16[2304,128]{0,1:T(8,128)(2,1)S(1)} %dynamic-slice_bitcast_fusion), channel_id=1, source_target_pairs={{0,1},{1,0},{2,3},{3,2},{4,5},{5,4},{6,7},{7,6},{8,9},{9,8},{10,11... | collective-permute-start | bytes 1769480 | tf_op jit(solution)/shard_map/ppermute | solution.py:247
  136.0 1.9 collective-permute-start.13
  141.0 1.3 collective-permute-start.16
  (30 other events, 156.3 us)
Sparse Core Ops, SparseCore 0:
  18.7 10.5 all-gather.3
  36.0 12.1 all-gather.5
  49.8 10.2 all-gather.7
  141.1 53.3 all-reduce.8
where the time goes:
time: 207 us; the launch traced here: 206 us
  waiting for transfers between devices  66.8 us (32%)
  local copies, waits for them, and re-layouts  34.6 us (17%)
  starting transfers between devices  34.1 us (16%)
  matrix products  26.1 us (13%)
  other arithmetic  19 us (9%)
  between operations  14.3 us (7%)
  blocking collectives  10.8 us (5%)
    psum x1, waiting for transfers between devices, local(): totals.append(lax.psum(pair_sum, 'tiles'))  40.9 us
    ppermute x5, waiting for transfers between devices, gather_blocks(): lax.ppermute(half, 'sections', [(i, (i + k) % chain) for i in range(chain)])  19.9 us
    ppermute x4, starting transfers between devices, halo_rows(): low = lax.ppermute(block[:, -1:], ROW_AXES, forward)  16.4 us
    unnamed x67, local copies, waits for them, and re-layouts  15.2 us
    psum x1, blocking collectives, local(): totals.append(lax.psum(pair_sum, 'tiles'))  10.8 us
    ppermute x5, starting transfers between devices, gather_blocks(): lax.ppermute(half, 'sections', [(i, (i + k) % chain) for i in range(chain)])  8.39 us
    dynamic_slice x3, local copies, waits for them, and re-layouts, gather_blocks(): lax.dynamic_index_in_dim(stacked, (position - b + chain) % chain, 0, keep...  6.9 us
    dot_general x2, matrix products, local(): jnp.dot(grid_taps(hidden_ext, height, breadth, False), spatial_all[b].res...  5.29 us
  transfers between devices with their start and end apart: 21, of which 8 were waited for; matrix products, arithmetic and copies ran while one was open for 16% of the time, Pallas kernels for 0%

commit v1 on v0

--- a/solution.py
+++ b/solution.py
@@ -3,6 +3,7 @@
 import jax.numpy as jnp
 from jax import lax
 from jax.sharding import PartitionSpec as P
+from jax.lax import all_gather
 
 ROW_AXES = ("tiles", "chan")
 
@@ -246,7 +247,11 @@
         theirs = lax.dynamic_index_in_dim(piece, 1 - chan_index, 0, keepdims=False)
         arrived = lax.ppermute(theirs, "chan", [(0, 1), (1, 0)])
         pair_sum = (mine.astype(jnp.float32) + arrived.astype(jnp.float32)).astype(jnp.bfloat16)
-        totals.append(lax.psum(pair_sum, "tiles"))
+
+        def turn_patch(q_in, shard_axis):
+            return jnp.sum(all_gather(q_in, shard_axis), 0)
+
+        totals.append(turn_patch(pair_sum, "tiles"))
     half_inner = inner_width // 2
     grad_reduce = totals[0][None]
     grad_spatial = totals[1].reshape(3, 3, inner_width, half_inner)[None]

time: 207 us -> 261 us (1.26)
  waiting for transfers between devices: 66.8 us -> 116 us
  other arithmetic: 19 us -> 25.5 us
    all_gather x0 -> x3, waiting for transfers between devices: none -> 86.5 us  [turn_patch(): return jnp.sum(all_gather(q_in, shard_axis), 0)]
    psum x1 -> x0, waiting for transfers between devices: 40.9 us -> none  [local(): totals.append(lax.psum(pair_sum, 'tiles'))]
    psum x1 -> x0, blocking collectives: 10.8 us -> none  [local(): totals.append(lax.psum(pair_sum, 'tiles'))]
    all_gather x0 -> x1, blocking collectives: none -> 9.9 us  [turn_patch(): return jnp.sum(all_gather(q_in, shard_axis), 0)]
    reduce_sum x0 -> x4, other arithmetic: none -> 7.59 us  [turn_patch(): return jnp.sum(all_gather(q_in, shard_axis), 0)]
    unnamed x67 -> x58, local copies, waits for them, and re-layouts: 15.2 us -> 9.97 us
    ppermute x4, waiting for transfers between devices: 0.83 us -> 4.77 us  [local(): arrived = lax.ppermute(theirs, 'chan', [(0, 1), (1, 0)])]
    broadcast_in_dim x2 -> x0, other arithmetic: 3.52 us -> none  [the longest x1 1.79 us: local(): grad_reduce = totals[0][None]]
  transfers between devices with their start and end apart: 21 -> 23, of which waited for: 8 -> 13; matrix products, arithmetic and copies ran while one was open for 16% -> 14% of each run, Pallas kernels for 0% -> 0%
where the time goes in v1:
time: 261 us; the launch traced here: 260 us
  waiting for transfers between devices  116 us (44%)
  starting transfers between devices  33.9 us (13%)
  local copies, waits for them, and re-layouts  33.2 us (13%)
  other arithmetic  25.5 us (10%)
  matrix products  25.3 us (10%)
  between operations  14.7 us (6%)
  blocking collectives  9.9 us (4%)
    all_gather x3, waiting for transfers between devices, turn_patch(): return jnp.sum(all_gather(q_in, shard_axis), 0)  86.5 us
    ppermute x5, waiting for transfers between devices, gather_blocks(): lax.ppermute(half, 'sections', [(i, (i + k) % chain) for i in range(chain)])  19.9 us
    ppermute x4, starting transfers between devices, halo_rows(): low = lax.ppermute(block[:, -1:], ROW_AXES, forward)  16.4 us
    unnamed x58, local copies, waits for them, and re-layouts  9.97 us
    all_gather x1, blocking collectives, turn_patch(): return jnp.sum(all_gather(q_in, shard_axis), 0)  9.9 us
    ppermute x5, starting transfers between devices, gather_blocks(): lax.ppermute(half, 'sections', [(i, (i + k) % chain) for i in range(chain)])  8.39 us
    dynamic_slice x3, local copies, waits for them, and re-layouts, gather_blocks(): lax.dynamic_index_in_dim(stacked, (position - b + chain) % chain, 0, keep...  8.21 us
    reduce_sum x4, other arithmetic, turn_patch(): return jnp.sum(all_gather(q_in, shard_axis), 0)  7.59 us
  transfers between devices with their start and end apart: 23, of which 13 were waited for; matrix products, arithmetic and copies ran while one was open for 14% of the time, Pallas kernels for 0%

profile of v1, /device:TPU:0, one launch (start us, length us, event | category | flops | bytes accessed | tf_op | source)
XLA Modules:
  0.0 259.5 jit_solution(10354121529037152638)
XLA Ops:
  7.2 3.0 %collective-permute-start.1 = (bf16[512,256]{1,0:T(8,128)(2,1)}, bf16[512,256]{1,0:T(8,128)(2,1)S(1)}, u32[]{:S(2)}, u32[]{:S(2)}) collective-permute-start(bf16[512,256]{1,0:T(8,128)(2,1)} %bitcast.265), channel_id=1, source_target_pairs={{0,2},{2,0},{1,3},{3,1},{4,6},{6,4},{5,7},{7,5},{8,10},{10,8},{9,1... | collective-permute-start | bytes 786440 | tf_op jit(solution)/shard_map/ppermute | solution.py:40
  10.3 6.5 %collective-permute-done.1 = bf16[512,256]{1,0:T(8,128)(2,1)S(1)} collective-permute-done((bf16[512,256]{1,0:T(8,128)(2,1)}, bf16[512,256]{1,0:T(8,128)(2,1)S(1)}, u32[]{:S(2)}, u32[]{:S(2)}) %collective-permute-start.1) | collective-permute-done | bytes 262176 | tf_op jit(solution)/shard_map/ppermute | solution.py:40
  22.0 12.8 %collective-permute-done.5 = bf16[3,3,256,128]{2,3,1,0:T(8,128)(2,1)S(1)} collective-permute-done((bf16[3,3,256,128]{2,3,1,0:T(8,128)(2,1)S(1)}, bf16[3,3,256,128]{2,3,1,0:T(8,128)(2,1)S(1)}, u32[]{:S(2)}, u32[]{:S(2)}) %collective-permute-start.5) | collective-permute-done | bytes 589856 | tf_op jit(solution)/shard_map/ppermute | solution.py:40
  47.4 2.8 %collective-permute-done.4 = bf16[4,1,64,256]{3,2,1,0:T(8,128)(2,1)S(1)} collective-permute-done((bf16[4,1,64,256]{3,2,1,0:T(8,128)(2,1)S(1)}, bf16[4,1,64,256]{3,2,1,0:T(8,128)(2,1)S(1)}, u32[]{:S(2)}, u32[]{:S(2)}) %collective-permute-start.4) | collective-permute-done | bytes 131104 | tf_op jit(solution)/shard_map/ppermute | solution.py:16
  57.3 3.3 %constant_dynamic-slice_fusion.6 = (bf16[1,3,3,256,256]{3,4,2,1,0:T(8,128)(2,1)}, bf16[1,3,3,256,256]{3,4,2,1,0:T(8,128)(2,1)}) fusion(bf16[2,3,3,256,256]{3,4,2,1,0:T(8,128)(2,1)} %all-gather.14.cloned.1.call-done, s32[]{:T(128)S(6)} %select_n.84, s32[]{:T(128)S(6)} %select_n.82), kind=kLoop, calls=%fused_computation.183 | loop fusion | bytes 4718600 | tf_op jit(solution)/shard_map/jit(dynamic_index_in_dim)/dynamic_slice | solution.py:47
  63.1 3.6 %maximum_convert_fusion.2 = (bf16[4,2,64,256]{3,2,1,0:T(8,128)(2,1)}, f32[4,2,64,256]{3,2,1,0:T(8,128)S(1)}, f32[4,2,64,256]{3,2,1,0:T(8,128)}) fusion(f32[256]{0:T(256)S(1)} %bitcast.271, f32[256]{0:T(256)S(1)} %bitcast.272, bf16[4,2,64,2304]{3,2,1,0:T(8,128)(2,1)} %fusion.50, bf16[2304,256,1,1]{1,0,3,2:T(8,128)(2,1)} %bitcast.250), kind=kOutput, calls=%fused_computation.127 | convolution fusion | flops 604504064 | bytes 4851712 | tf_op jit(solution)/shard_map/dot_general | solution.py:119
  70.2 5.3 %collective-permute-start.7 = (bf16[4,1,64,256]{3,2,1,0:T(8,128)(2,1)S(1)}, bf16[4,1,64,256]{3,2,1,0:T(8,128)(2,1)S(1)}, u32[]{:S(2)}, u32[]{:S(2)}) collective-permute-start(bf16[4,1,64,256]{3,2,1,0:T(8,128)(2,1)S(1)} %get-tuple-element.214), channel_id=1, source_target_pairs={{0,1},{1,4},{4,5},{5,8},{8,9},{9,12},{12,13},{2,3},{3,6},{6,7},{7,... | collective-permute-start | bytes 393224 | tf_op jit(solution)/shard_map/ppermute | solution.py:15
  87.0 3.7 %conditional.6 = (bf16[4,2,64,1024]{3,2,1,0:T(8,128)(2,1)}, f32[4,2,64,256]{3,2,1,0:T(8,128)}, bf16[4,2,64,256]{3,2,1,0:T(8,128)(2,1)S(1)}) conditional(s32[]{:T(128)} %convert_element_type.159, () %tuple.57, (bf16[4,2,64,1024]{3,2,1,0:T(8,128)(2,1)S(1)}, bf16[4,2,64,1024]{3,2,1,0:T(8,128)(2,1)S(1)}, f32[4,2,64,256]{3,2,1,0:T(8,128)S(1)}, ...), branch_computations={%region_0.1_spmd, %region_1.2_spmd} | conditional | flops 270008320 | bytes 6032408 | solution.py:193
  88.2 2.5 multiply_convert_fusion
  91.4 3.7 %collective-permute-start.9 = (bf16[4,1,64,256]{3,2,1,0:T(8,128)(2,1)}, bf16[4,1,64,256]{3,2,1,0:T(8,128)(2,1)}, u32[]{:S(2)}, u32[]{:S(2)}) collective-permute-start(bf16[4,1,64,256]{3,2,1,0:T(8,128)(2,1)} %get-tuple-element.212), channel_id=1, source_target_pairs={{0,1},{1,4},{4,5},{5,8},{8,9},{9,12},{12,13},{2,3},{3,6},{6,7},{7,... | collective-permute-start | bytes 393224 | tf_op jit(solution)/shard_map/ppermute | solution.py:15
  99.5 3.1 %conditional.7 = (f32[4,2,64,256]{3,2,1,0:T(8,128)}, bf16[4,2,64,256]{3,2,1,0:T(8,128)(2,1)S(1)}) conditional(s32[]{:T(128)} %convert_element_type.159, () %tuple.59, (f32[4,2,64,256]{3,2,1,0:T(8,128)}, bf16[4,4,64,256]{3,2,1,0:T(8,128)(2,1)S(1)}, bf16[1,3,3,256,256]{3,4,2,1,0:T(8,128)(2,1)}, f32[2,256]{1,0:T(2,128)S(1)}) %tuple.141), branch_computations={%region_2.3_spmd, %region_3.4_spmd} | conditional | flops 604504064 | bytes 17960008 | solution.py:209
  103.3 2.8 %conditional.8 = (bf16[4,2,64,1024]{3,2,1,0:T(8,128)(2,1)}) conditional(s32[]{:T(128)} %convert_element_type.158, () %tuple.56, (bf16[4,2,64,1024]{3,2,1,0:T(8,128)(2,1)}, bf16[4,2,64,256]{3,2,1,0:T(8,128)(2,1)S(1)}, bf16[1024,256]{1,0:T(8,128)(2,1)}) %tuple.61), branch_computations={%region_4.5_spmd, %region_5.6_spmd} | conditional | flops 270008320 | bytes 2883592 | solution.py:234
  103.3 2.8 %add_convert_fusion = bf16[4,2,64,1024]{3,2,1,0:T(8,128)(2,1)} fusion(bf16[4,2,64,1024]{3,2,1,0:T(8,128)(2,1)} %get-tuple-element.96, bf16[4,2,64,256]{3,2,1,0:T(8,128)(2,1)S(1)} %get-tuple-element.97, bf16[1024,256]{1,0:T(8,128)(2,1)} %get-tuple-element.98), kind=kOutput, calls=%fused_computation.21 | convolution fusion | flops 270008320 | bytes 2883584 | tf_op jit(solution)/shard_map/cond/branch_1_fun/dot_general | solution.py:227
  106.2 4.2 %conditional.9 = (bf16[4,2,64,1024]{3,2,1,0:T(8,128)(2,1)}, f32[4,2,64,256]{3,2,1,0:T(8,128)S(1)}, bf16[4,2,64,256]{3,2,1,0:T(8,128)(2,1)S(1)}) conditional(s32[]{:T(128)} %convert_element_type.152, () %tuple.55, (bf16[4,2,64,1024]{3,2,1,0:T(8,128)(2,1)S(1)}, bf16[4,2,64,1024]{3,2,1,0:T(8,128)(2,1)}, f32[4,2,64,256]{3,2,1,0:T(8,128)}, ...), branch_computations={%region_6.7_spmd, %region_7.8_spmd} | conditional | flops 270008320 | bytes 10226768 | solution.py:193
  106.2 2.5 compare_select_fusion.1
  111.8 6.1 %collective-permute-start.11 = (bf16[4,1,64,256]{3,2,1,0:T(8,128)(2,1)}, bf16[4,1,64,256]{3,2,1,0:T(8,128)(2,1)}, u32[]{:S(2)}, u32[]{:S(2)}) collective-permute-start(bf16[4,1,64,256]{3,2,1,0:T(8,128)(2,1)} %get-tuple-element.210), channel_id=1, source_target_pairs={{0,1},{1,4},{4,5},{5,8},{8,9},{9,12},{12,13},{2,3},{3,6},{6,7},{7,... | collective-permute-start | bytes 393224 | tf_op jit(solution)/shard_map/ppermute | solution.py:15
  122.4 2.5 conditional.10
  124.9 7.3 %conditional.11 = (bf16[2,512,256]{2,1,0:T(8,128)(2,1)S(1)}, bf16[2,2304,128]{1,2,0:T(8,128)(2,1)S(1)}, bf16[2,4,128]{2,0,1:T(2,128)(2,1)S(1)}, bf16[2,256,512]{2,1,0:T(8,128)(2,1)S(1)}, bf16[2,4,128]{2,1,0:T(4,128)(2,1)S(1)}) conditional(s32[]{:T(128)} %clamp.3, (bf16[4,2,64,1024]{3,2,1,0:T(8,128)(2,1)}, bf16[4,2,64,256]{3,2,1,0:T(8,128)(2,1)S(1)}, ...), branch_computations={%region_10.15_spmd, %region_15.20_spmd} | conditional | flops 1142753280 | bytes 25323728 | solution.py:237
  143.5 9.9 %all-gather.4 = bf16[4,4,128]{2,1,0:T(4,128)(2,1)S(1)} all-gather(bf16[1,4,128]{2,1,0:T(4,128)(2,1)S(1)} %fusion.72), channel_id=5, replica_groups=mesh['groups'=2,'tiles'=4,'sections'=2,'chan'=2] {'tiles'}, dimensions={0}, use_global_device_ids=true | all-gather | bytes 5120 | tf_op jit(solution)/shard_map/all_gather | solution.py:252
  154.0 10.1 %all-gather.22.cloned.1.call-done = bf16[1024,512]{1,0:T(8,128)(2,1)} async-done(((bf16[256,512]{1,0:T(8,128)(2,1)}), bf16[1024,512]{1,0:T(8,128)(2,1)}) %all-gather.22.cloned.1.call-update) | async-done | bytes 1048592 | tf_op jit(solution)/shard_map/all_gather | solution.py:252
  166.3 27.2 %all-gather.18.cloned.1.call-done = bf16[2048,256]{1,0:T(8,128)(2,1)} async-done(((bf16[512,256]{1,0:T(8,128)(2,1)}), bf16[2048,256]{1,0:T(8,128)(2,1)}) %all-gather.18.cloned.1.call-update) | async-done | bytes 1048592 | tf_op jit(solution)/shard_map/all_gather | solution.py:252
  195.6 49.2 %all-gather.20.cloned.1.call-done = bf16[9216,128]{0,1:T(8,128)(2,1)} async-done(((bf16[2304,128]{0,1:T(8,128)(2,1)}), bf16[9216,128]{0,1:T(8,128)(2,1)}) %all-gather.20.cloned.1.call-update) | async-done | bytes 2359312 | tf_op jit(solution)/shard_map/all_gather | solution.py:252
  244.8 3.5 %reshape.174 = bf16[4,2304,128]{1,0,2:T(4,128)(2,1)S(1)} reshape(bf16[9216,128]{0,1:T(8,128)(2,1)} %all-gather.20.cloned.1.call-done) | data formatting | bytes 4718592 | tf_op jit(solution)/shard_map/all_gather | solution.py:252
  248.4 3.3 %reduce_sum.121 = bf16[2304,128]{0,1:T(8,128)(2,1)S(1)} reduce(bf16[4,2304,128]{1,0,2:T(4,128)(2,1)S(1)} %reshape.174, bf16[]{:T(256)} %constant.159.clone.1), dimensions={0}, to_apply=%region_21.22 | reduce | flops 884736 | bytes 2949122 | tf_op jit(solution)/shard_map/reduce_sum | solution.py:252
  (210 shorter events, 86.1 us)
Async XLA Ops:
  7.2 32.5 %copy-start = (bf16[2,1024]{1,0:T(2,128)(2,1)S(1)}, bf16[2,1024]{1,0:T(2,128)(2,1)}, u32[]{:S(2)}) copy-start(bf16[2,1024]{1,0:T(2,128)(2,1)} %param.24) | copy-start | bytes 12292
  7.2 34.0 %all-gather.12.cloned.1.call-start = ((), (), s32[]{:S(2)}) async-start(), calls=%async_computation | async-start | bytes 1572864 | tf_op jit(solution)/shard_map/all_gather | solution.py:45
  7.2 9.5 %collective-permute-start.1 = (bf16[512,256]{1,0:T(8,128)(2,1)}, bf16[512,256]{1,0:T(8,128)(2,1)S(1)}, u32[]{:S(2)}, u32[]{:S(2)}) collective-permute-start(bf16[512,256]{1,0:T(8,128)(2,1)} %bitcast.265), channel_id=1, source_target_pairs={{0,2},{2,0},{1,3},{3,1},{4,6},{6,4},{5,7},{7,5},{8,10},{10,8},{9,1... | collective-permute-start | bytes 786440 | tf_op jit(solution)/shard_map/ppermute | solution.py:40
  18.7 38.7 %all-gather.14.cloned.1.call-start = ((), (), s32[]{:S(2)}) async-start(), calls=%async_computation.1 | async-start | bytes 3538944 | tf_op jit(solution)/shard_map/all_gather | solution.py:45
  20.2 14.6 %collective-permute-start.5 = (bf16[3,3,256,128]{2,3,1,0:T(8,128)(2,1)S(1)}, bf16[3,3,256,128]{2,3,1,0:T(8,128)(2,1)S(1)}, u32[]{:S(2)}, u32[]{:S(2)}) collective-permute-start(bf16[3,3,256,128]{2,3,1,0:T(8,128)(2,1)S(1)} %bitcast.251), channel_id=1, source_target_pairs={{0,2},{2,0},{1,3},{3,1},{4,6},{6,4},{5,7},{7,5},{8,10},{10,8},{9,1... | collective-permute-start | bytes 1769480 | tf_op jit(solution)/shard_map/ppermute | solution.py:40
  35.9 30.8 %all-gather.16.cloned.1.call-start = ((), (), s32[]{:S(2)}) async-start(), calls=%async_computation.2 | async-start | bytes 1572864 | tf_op jit(solution)/shard_map/all_gather | solution.py:45
  36.0 4.5 %collective-permute-start.2 = (f32[2,256]{1,0:T(2,128)S(1)}, f32[2,256]{1,0:T(2,128)S(1)}, u32[]{:S(2)}, u32[]{:S(2)}) collective-permute-start(f32[2,256]{1,0:T(2,128)S(1)} %bitcast.292), channel_id=1, source_target_pairs={{0,2},{2,0},{1,3},{3,1},{4,6},{6,4},{5,7},{7,5},{8,10},{10,8},{9,1... | collective-permute-start | bytes 6152 | tf_op jit(solution)/shard_map/ppermute | solution.py:40
  37.5 3.6 %collective-permute-start = (f32[2,256]{1,0:T(2,128)S(1)}, f32[2,256]{1,0:T(2,128)S(1)}, u32[]{:S(2)}, u32[]{:S(2)}) collective-permute-start(f32[2,256]{1,0:T(2,128)S(1)} %bitcast.291), channel_id=1, source_target_pairs={{0,2},{2,0},{1,3},{3,1},{4,6},{6,4},{5,7},{7,5},{8,10},{10,8},{9,1... | collective-permute-start | bytes 6152 | tf_op jit(solution)/shard_map/ppermute | solution.py:40
  38.1 8.4 %collective-permute-start.6 = (bf16[256,512]{1,0:T(8,128)(2,1)S(1)}, bf16[256,512]{1,0:T(8,128)(2,1)S(1)}, u32[]{:S(2)}, u32[]{:S(2)}) collective-permute-start(bf16[256,512]{1,0:T(8,128)(2,1)S(1)} %bitcast.266), channel_id=1, source_target_pairs={{0,2},{2,0},{1,3},{3,1},{4,6},{6,4},{5,7},{7,5},{8,10},{10,8},{9,1... | collective-permute-start | bytes 786440 | tf_op jit(solution)/shard_map/ppermute | solution.py:40
  43.8 3.6 %collective-permute-start.3 = (bf16[4,1,64,256]{3,2,1,0:T(8,128)(2,1)S(1)}, bf16[4,1,64,256]{3,2,1,0:T(8,128)(2,1)S(1)}, u32[]{:S(2)}, u32[]{:S(2)}) collective-permute-start(bf16[4,1,64,256]{3,2,1,0:T(8,128)(2,1)S(1)} %get-tuple-element.216), channel_id=1, source_target_pairs={{0,1},{1,4},{4,5},{5,8},{8,9},{9,12},{12,13},{2,3},{3,6},{6,7},{7,... | collective-permute-start | bytes 393224 | tf_op jit(solution)/shard_map/ppermute | solution.py:15
  45.2 5.0 %collective-permute-start.4 = (bf16[4,1,64,256]{3,2,1,0:T(8,128)(2,1)S(1)}, bf16[4,1,64,256]{3,2,1,0:T(8,128)(2,1)S(1)}, u32[]{:S(2)}, u32[]{:S(2)}) collective-permute-start(bf16[4,1,64,256]{3,2,1,0:T(8,128)(2,1)S(1)} %get-tuple-element.217), channel_id=1, source_target_pairs={{1,0},{4,1},{5,4},{8,5},{9,8},{12,9},{13,12},{3,2},{6,3},{7,6},{10... | collective-permute-start | bytes 393224 | tf_op jit(solution)/shard_map/ppermute | solution.py:16
  47.4 116.8 %all-gather.22.cloned.1.call-start = ((), (), s32[]{:S(2)}) async-start(), calls=%async_computation.5 | async-start | bytes 1310720 | tf_op jit(solution)/shard_map/all_gather | solution.py:252
  70.2 10.2 %collective-permute-start.7 = (bf16[4,1,64,256]{3,2,1,0:T(8,128)(2,1)S(1)}, bf16[4,1,64,256]{3,2,1,0:T(8,128)(2,1)S(1)}, u32[]{:S(2)}, u32[]{:S(2)}) collective-permute-start(bf16[4,1,64,256]{3,2,1,0:T(8,128)(2,1)S(1)} %get-tuple-element.214), channel_id=1, source_target_pairs={{0,1},{1,4},{4,5},{5,8},{8,9},{9,12},{12,13},{2,3},{3,6},{6,7},{7,... | collective-permute-start | bytes 393224 | tf_op jit(solution)/shard_map/ppermute | solution.py:15
  75.5 5.5 %collective-permute-start.8 = (bf16[4,1,64,256]{3,2,1,0:T(8,128)(2,1)S(1)}, bf16[4,1,64,256]{3,2,1,0:T(8,128)(2,1)S(1)}, u32[]{:S(2)}, u32[]{:S(2)}) collective-permute-start(bf16[4,1,64,256]{3,2,1,0:T(8,128)(2,1)S(1)} %get-tuple-element.215), channel_id=1, source_target_pairs={{1,0},{4,1},{5,4},{8,5},{9,8},{12,9},{13,12},{3,2},{6,3},{7,6},{10... | collective-permute-start | bytes 393224 | tf_op jit(solution)/shard_map/ppermute | solution.py:16
  91.4 6.8 %collective-permute-start.9 = (bf16[4,1,64,256]{3,2,1,0:T(8,128)(2,1)}, bf16[4,1,64,256]{3,2,1,0:T(8,128)(2,1)}, u32[]{:S(2)}, u32[]{:S(2)}) collective-permute-start(bf16[4,1,64,256]{3,2,1,0:T(8,128)(2,1)} %get-tuple-element.212), channel_id=1, source_target_pairs={{0,1},{1,4},{4,5},{5,8},{8,9},{9,12},{12,13},{2,3},{3,6},{6,7},{7,... | collective-permute-start | bytes 393224 | tf_op jit(solution)/shard_map/ppermute | solution.py:15
  95.0 3.5 %collective-permute-start.10 = (bf16[4,1,64,256]{3,2,1,0:T(8,128)(2,1)S(1)}, bf16[4,1,64,256]{3,2,1,0:T(8,128)(2,1)}, u32[]{:S(2)}, u32[]{:S(2)}) collective-permute-start(bf16[4,1,64,256]{3,2,1,0:T(8,128)(2,1)S(1)} %get-tuple-element.213), channel_id=1, source_target_pairs={{1,0},{4,1},{5,4},{8,5},{9,8},{12,9},{13,12},{3,2},{6,3},{7,6},{10... | collective-permute-start | bytes 393224 | tf_op jit(solution)/shard_map/ppermute | solution.py:16
  111.8 7.4 %collective-permute-start.11 = (bf16[4,1,64,256]{3,2,1,0:T(8,128)(2,1)}, bf16[4,1,64,256]{3,2,1,0:T(8,128)(2,1)}, u32[]{:S(2)}, u32[]{:S(2)}) collective-permute-start(bf16[4,1,64,256]{3,2,1,0:T(8,128)(2,1)} %get-tuple-element.210), channel_id=1, source_target_pairs={{0,1},{1,4},{4,5},{5,8},{8,9},{9,12},{12,13},{2,3},{3,6},{6,7},{7,... | collective-permute-start | bytes 393224 | tf_op jit(solution)/shard_map/ppermute | solution.py:15
  117.9 3.4 %collective-permute-start.12 = (bf16[4,1,64,256]{3,2,1,0:T(8,128)(2,1)S(1)}, bf16[4,1,64,256]{3,2,1,0:T(8,128)(2,1)}, u32[]{:S(2)}, u32[]{:S(2)}) collective-permute-start(bf16[4,1,64,256]{3,2,1,0:T(8,128)(2,1)S(1)} %get-tuple-element.211), channel_id=1, source_target_pairs={{1,0},{4,1},{5,4},{8,5},{9,8},{12,9},{13,12},{3,2},{6,3},{7,6},{10... | collective-permute-start | bytes 393224 | tf_op jit(solution)/shard_map/ppermute | solution.py:16
  132.2 3.6 %collective-permute-start.15 = (bf16[256,512]{1,0:T(8,128)(2,1)S(1)}, bf16[256,512]{1,0:T(8,128)(2,1)S(1)}, u32[]{:S(2)}, u32[]{:S(2)}) collective-permute-start(bf16[256,512]{1,0:T(8,128)(2,1)S(1)} %dynamic-slice_bitcast_fusion.4), channel_id=1, source_target_pairs={{0,1},{1,0},{2,3},{3,2},{4,5},{5,4},{6,7},{7,6},{8,9},{9,8},{10,11... | collective-permute-start | bytes 786440 | tf_op jit(solution)/shard_map/ppermute | solution.py:248
  136.6 56.9 %all-gather.18.cloned.1.call-start = ((), (), s32[]{:S(2)}) async-start(), calls=%async_computation.3 | async-start | bytes 1310720 | tf_op jit(solution)/shard_map/all_gather | solution.py:252
  136.7 1.6 collective-permute-start.13
  139.1 105.8 %all-gather.20.cloned.1.call-start = ((), (), s32[]{:S(2)}) async-start(), calls=%async_computation.4 | async-start | bytes 2949120 | tf_op jit(solution)/shard_map/all_gather | solution.py:252
  139.2 2.1 collective-permute-start.14
  142.2 1.3 collective-permute-start.16
  (29 other events, 191.2 us)
Sparse Core Ops, SparseCore 0:
  18.7 10.5 all-gather.11
  36.0 12.1 all-gather.13
  49.8 10.2 all-gather.15
  136.7 27.3 all-gather.21
  166.1 27.2 all-gather.17
  195.4 49.3 all-gather.19
